TPU v7x, 256 devices: a whole 4x4x8 slice. The times are simulated.
256 devices in a mesh: dp: 8 (over y, x_hi), expert: 8 (over z), tensor: 4 (over x_lo, core).
Axes of the slice: x: 4 (x_hi: 2, x_lo: 2; x = x_hi * 2 + x_lo), y: 4, z: 8, core: 2. Of those that a mesh axis runs over, the one named last changes fastest.
Arguments:
- tokens: bfloat16 [4096, 2048], P(('dp', 'expert', 'tensor')), may hold values from -6 to 6
- cotangent: bfloat16 [4096, 2048], P(('dp', 'expert', 'tensor')), may hold values from -3 to 3
- routes: int32 [4096, 2], P(('dp', 'expert', 'tensor')), may hold values from 0 to 7, all different within a row; in each aligned block of 16 rows (0 to 15, 16 to 31, ...) at most 5 rows name the same one
- weight_codes: int32 [4096, 2], P(('dp', 'expert', 'tensor')), may hold values from 16 to 256
- dense_gate: bfloat16 [2048, 8192], P('expert', ('dp', 'tensor')), may hold values from -0.125 to 0.125
- dense_up: bfloat16 [2048, 8192], P('expert', ('dp', 'tensor')), may hold values from -0.125 to 0.125
- dense_down_t: bfloat16 [2048, 8192], P('expert', ('dp', 'tensor')), may hold values from -0.0625 to 0.0625
Outputs:
- mixed: bfloat16 [4096, 2048], P(('dp', 'expert', 'tensor'))
- input_grad: bfloat16 [4096, 2048], P(('dp', 'expert', 'tensor'))
- grad_gate: bfloat16 [8, 2048, 8192], P('expert', None, ('dp', 'tensor'))
- grad_up: bfloat16 [8, 2048, 8192], P('expert', None, ('dp', 'tensor'))
- grad_down_t: bfloat16 [8, 2048, 8192], P('expert', None, ('dp', 'tensor'))
Inputs may be any that keep to these rules, and one draw needn't show every extreme that they name: `routes`: each row names two different experts; the rows of one device name each expert at most 5 times.
All inputs are finite; a program needn't handle non-finite values.
Results may differ from a plain program's by a relative error of at most 0.02.
Values may be sent and summed in bfloat16 or wider, within the bound.
No kernel may reach another device: no remote copies, remote signals or barrier semaphores. Data moves between devices by JAX's collectives and lax.ppermute only.
A program may use at most 128 MiB of HBM per device.

v0:
```python
import jax
import jax.numpy as jnp
from jax import lax
from jax.sharding import PartitionSpec as P

GROUP = ("dp", "tensor")


def silu_parts(gate_pre):
    sigmoid_val = jax.nn.sigmoid(gate_pre)
    return (gate_pre * sigmoid_val, sigmoid_val * (1.0 + gate_pre * (1.0 - sigmoid_val)))


def contract_rows(left_side, right_side):
    return lax.dot_general(
        left_side, right_side, (((0,), (0,)), ((), ())), preferred_element_type=jnp.float32
    )


def contract_cols(left_side, right_side):
    return lax.dot_general(
        left_side, right_side, (((1,), (1,)), ((), ())), preferred_element_type=jnp.float32
    )


def forward_parts(rows_x, gate_cols, up_cols):
    gate_pre = jnp.dot(rows_x, gate_cols, preferred_element_type=jnp.float32)
    up_pre = jnp.dot(rows_x, up_cols, preferred_element_type=jnp.float32)
    activation, act_slope = silu_parts(gate_pre)
    hidden = (activation * up_pre).astype(jnp.bfloat16)
    return (up_pre, activation, act_slope, hidden)


def grad_parts(scaled, down_cols, up_pre, activation, act_slope):
    hidden_grad = jnp.dot(scaled, down_cols, preferred_element_type=jnp.float32)
    gate_grad = (hidden_grad * up_pre * act_slope).astype(jnp.bfloat16)
    up_grad = (hidden_grad * activation).astype(jnp.bfloat16)
    return (gate_grad, up_grad)


def shards(tokens, cotangent, routes, weight_codes, dense_gate, dense_up, dense_down_t):
    experts = lax.axis_size("expert")
    count_tok, model_width = tokens.shape
    hid = dense_gate.shape[1]
    capacity = 5 * count_tok // (2 * experts)
    slots_here = experts * capacity
    stacked = jnp.concatenate([dense_gate, dense_up, dense_down_t], axis=1)
    full_cols = lax.all_gather(stacked, "expert", axis=0, tiled=True)
    gate_cols = full_cols[:, :hid]
    up_cols = full_cols[:, hid : 2 * hid]
    down_cols = full_cols[:, 2 * hid :]
    gate_up_cols = full_cols[:, : 2 * hid]
    code_cols = jnp.zeros((count_tok, 128), jnp.bfloat16)
    code_cols = code_cols.at[:, 0:2].set(weight_codes.astype(jnp.bfloat16))
    home = jnp.concatenate([tokens, cotangent, code_cols], axis=1)
    plane = lax.all_gather(home, GROUP, axis=0, tiled=True)
    plane_x = plane[:, :model_width]
    plane_dy = plane[:, model_width : 2 * model_width].astype(jnp.float32)
    plane_scale = plane[:, 2 * model_width : 2 * model_width + 2].astype(jnp.float32) / 256.0
    up_pre, activation, act_slope, hidden = forward_parts(plane_x, gate_cols, up_cols)
    out_term = contract_cols(hidden, down_cols).astype(jnp.bfloat16)
    grad_term = jnp.zeros(out_term.shape, jnp.float32)
    for which in range(2):
        scaled = (plane_scale[:, which : which + 1] * plane_dy).astype(jnp.bfloat16)
        gate_grad, up_grad = grad_parts(scaled, down_cols, up_pre, activation, act_slope)
        grad_term = grad_term + contract_cols(
            jnp.concatenate([gate_grad, up_grad], axis=1), gate_up_cols
        )
    terms = jnp.concatenate([out_term, grad_term.astype(jnp.bfloat16)], axis=1)
    summed = lax.psum_scatter(terms, GROUP, scatter_dimension=0, tiled=True)
    expert_out = summed[:, :model_width].astype(jnp.float32)
    code_scale = weight_codes.astype(jnp.float32) / 256.0
    mixed = (code_scale[:, 0:1] * expert_out + code_scale[:, 1:2] * expert_out).astype(jnp.bfloat16)
    input_grad = summed[:, model_width:]
    flat_route = routes.reshape(-1)
    flat_scale = weight_codes.reshape(-1).astype(jnp.float32) / 256.0
    onehot = (flat_route[:, None] == jnp.arange(experts, dtype=jnp.int32)[None, :]).astype(
        jnp.int32
    )
    earlier = jnp.cumsum(onehot, axis=0) - onehot
    slot_of = flat_route * capacity + jnp.sum(earlier * onehot, axis=1)
    placed = (slot_of[None, :] == jnp.arange(slots_here, dtype=jnp.int32)[:, None]).astype(
        jnp.bfloat16
    )
    flat_x = jnp.repeat(tokens, 2, axis=0)
    flat_scaled = (
        flat_scale[:, None] * jnp.repeat(cotangent, 2, axis=0).astype(jnp.float32)
    ).astype(jnp.bfloat16)
    send_x = jnp.dot(placed, flat_x, preferred_element_type=jnp.float32).astype(jnp.bfloat16)
    send_s = jnp.dot(placed, flat_scaled, preferred_element_type=jnp.float32).astype(jnp.bfloat16)
    send = jnp.stack(
        [
            send_x.reshape(experts, capacity, model_width),
            send_s.reshape(experts, capacity, model_width),
        ],
        axis=1,
    )
    got = lax.all_to_all(send, "expert", split_axis=0, concat_axis=0, tiled=True)
    got = jnp.transpose(got, (1, 0, 2, 3))
    rows = lax.all_gather(got, GROUP, axis=1, tiled=True)
    rows_x = rows[0].reshape(-1, model_width)
    rows_s = rows[1].reshape(-1, model_width)
    r_up, r_act, r_slope, r_hidden = forward_parts(rows_x, gate_cols, up_cols)
    r_gate, r_upg = grad_parts(rows_s, down_cols, r_up, r_act, r_slope)
    grad_gate = contract_rows(rows_x, r_gate).astype(jnp.bfloat16)[None]
    grad_up = contract_rows(rows_x, r_upg).astype(jnp.bfloat16)[None]
    grad_down_t = contract_rows(rows_s, r_hidden).astype(jnp.bfloat16)[None]
    return (mixed, input_grad, grad_gate, grad_up, grad_down_t)


def solution(mesh):
    rows = P(("dp", "expert", "tensor"), None)
    weights = P("expert", ("dp", "tensor"))
    grads = P("expert", None, ("dp", "tensor"))
    return jax.shard_map(
        shards,
        mesh=mesh,
        in_specs=(rows, rows, rows, rows, weights, weights, weights),
        out_specs=(rows, rows, grads, grads, grads),
        check_vma=False,
    )
```

profile of v0, /device:TPU:1, one launch (start us, length us, event | category | flops | bytes accessed | tf_op | source)
XLA Modules:
  0.0 376.8 jit_solution(17290189949668021922)
XLA Ops:
  7.9 1.3 broadcast_select_fusion
  9.3 1.5 fusion.43
  10.9 1.8 pad_maximum_fusion.2
  12.8 54.0 %all-gather.4.cloned.1.call-done = bf16[512,4224]{1,0:T(8,128)(2,1)} async-done(((bf16[16,4224]{1,0:T(8,128)(2,1)}), bf16[512,4224]{1,0:T(8,128)(2,1)}) %all-gather.4.cloned.1.call-update) | async-done | bytes 4325392 | tf_op jit(solution)/shard_map/all_gather | solution.py:56
  68.0 44.9 %all-gather.6.cloned.1.call-done = bf16[2048,768]{1,0:T(8,128)(2,1)} async-done(((bf16[256,768]{1,0:T(8,128)(2,1)}), bf16[2048,768]{1,0:T(8,128)(2,1)}) %all-gather.6.cloned.1.call-update) | async-done | bytes 3145744 | tf_op jit(solution)/shard_map/all_gather | solution.py:48
  112.9 2.8 fusion.16
  115.8 2.5 fusion.18
  123.9 2.6 pad_maximum_fusion
  128.9 1.9 convolution_convert_fusion.4
  134.3 1.7 stack_reshape.6
  137.4 15.5 %all_to_all.5 = bf16[8,2,5,2048]{3,1,2,0:T(2,128)(2,1)} all-to-all(bf16[8,2,5,2048]{3,1,2,0:T(2,128)(2,1)S(1)} %copy.25), channel_id=1, replica_groups=mesh['dp'=8,'expert'=8,'tensor'=4] {'expert'}, dimensions={0} | all-to-all | bytes 655360 | tf_op jit(solution)/shard_map/all_to_all | solution.py:98
  152.9 60.5 %reduce-scatter.2.cloned.1.call-done = bf16[16,4096]{1,0:T(8,128)(2,1)} async-done(((bf16[512,4096]{1,0:T(8,128)(2,1)}), bf16[16,4096]{1,0:T(8,128)(2,1)}) %reduce-scatter.2.cloned.1.call-update) | async-done | bytes 131088 | tf_op jit(solution)/shard_map/reduce_scatter | solution.py:70
  213.4 1.5 slice.86
  214.9 1.5 multiply_convert_fusion.14
  216.5 64.0 %all-gather.8.cloned.1.call-done = bf16[2,256,5,2048]{3,0,2,1:T(2,128)(2,1)} async-done(((bf16[2,8,5,2048]{3,0,2,1:T(2,128)(2,1)}), bf16[2,256,5,2048]{3,0,2,1:T(2,128)(2,1)}) %all-gather.8.cloned.1.call-update) | async-done | bytes 10485776 | tf_op jit(solution)/shard_map/all_gather | solution.py:100
  280.5 53.6 %slice_reduce_fusion = (bf16[256,5,2048]{2,1,0:T(8,128)(2,1)}, bf16[256,5,2048]{2,1,0:T(8,128)(2,1)}) fusion(bf16[2,256,5,2048]{3,0,2,1:T(2,128)(2,1)} %all-gather.8.cloned.1.call-done), kind=kLoop, calls=%fused_computation | loop fusion | bytes 20971520 | tf_op jit(solution)/shard_map/slice | solution.py:102
  334.1 10.0 %reshape_squeeze.6 = bf16[1280,2048]{1,0:T(8,128)(2,1)} reshape(bf16[256,5,2048]{2,1,0:T(8,128)(2,1)} %get-tuple-element.18) | data formatting | bytes 10485760 | tf_op jit(solution)/shard_map/reshape;squeeze | solution.py:101
  344.2 10.0 %reshape_squeeze.7 = bf16[1280,2048]{1,0:T(8,128)(2,1)} reshape(bf16[256,5,2048]{2,1,0:T(8,128)(2,1)} %get-tuple-element.17) | data formatting | bytes 10485760 | tf_op jit(solution)/shard_map/reshape;squeeze | solution.py:102
  354.2 4.2 %fusion.24 = f32[1280,256]{1,0:T(8,128)S(1)} fusion(bf16[1280,2048]{1,0:T(8,128)(2,1)} %reshape_squeeze.6, bf16[2048,768]{1,0:T(8,128)(2,1)S(1)} %copy-done.1), kind=kOutput, calls=%fused_computation.38 | convolution fusion | flops 1342177280 | bytes 7602176 | tf_op jit(solution)/shard_map/dot_general | solution.py:27
  358.4 1.6 fusion.21
  360.0 2.9 fusion.4
  362.8 1.6 fusion.27
  364.4 2.9 fusion.3
  367.3 3.0 fusion.2
  (54 shorter events, 15.2 us)
Async XLA Ops:
  7.2 59.6 %all-gather.4.cloned.1.call-start = ((), (), s32[]{:S(2)}) async-start(), calls=%async_computation.2 | async-start | bytes 4460544 | tf_op jit(solution)/shard_map/all_gather | solution.py:56
  10.8 102.1 %all-gather.6.cloned.1.call-start = ((), (), s32[]{:S(2)}) async-start(), calls=%async_computation.3 | async-start | bytes 3538944 | tf_op jit(solution)/shard_map/all_gather | solution.py:48
  12.7 200.7 %reduce-scatter.2.cloned.1.call-start = ((), (), s32[]{:S(2)}) async-start(), calls=%async_computation.4 | async-start | bytes 4325376 | tf_op jit(solution)/shard_map/reduce_scatter | solution.py:70
  112.9 2.9 copy-start.1
  115.8 2.9 copy-start.5
  126.5 0.7 copy-start.6
  126.5 0.9 copy-start.4
  126.5 1.0 copy-start.2
  126.5 5.2 %copy-start.3 = (bf16[16,2048]{1,0:T(8,128)(2,1)S(1)}, bf16[16,2048]{1,0:T(8,128)(2,1)}, u32[]{:S(2)}) copy-start(bf16[16,2048]{1,0:T(8,128)(2,1)} %param.9) | copy-start | bytes 196612
  126.5 154.0 %all-gather.8.cloned.1.call-start = ((), (), s32[]{:S(2)}) async-start(), calls=%async_computation.5 | async-start | bytes 10813440 | tf_op jit(solution)/shard_map/all_gather | solution.py:100
  354.2 4.2 %copy-start = (bf16[1280,2048]{1,0:T(8,128)(2,1)S(1)}, bf16[1280,2048]{1,0:T(8,128)(2,1)}, u32[]{:S(2)}) copy-start(bf16[1280,2048]{1,0:T(8,128)(2,1)} %reshape_squeeze.6) | copy-start | bytes 15728644
  354.2 5.8 %slice-start = ((s8[5242880]{0:T(1024)(128)(4,1)}), s8[4194304]{0:T(1024)(128)(4,1)S(1)}, s32[]{:S(2)}) async-start(s8[5242880]{0:T(1024)(128)(4,1)} %bitcast.16), calls=%async_computation.6 | async-start | bytes 8388608
  358.4 1.6 slice-start.1
Sparse Core Ops, SparseCore 0:
  11.2 55.5 all-gather.3
  69.1 43.7 all-gather.5
  126.7 86.7 reduce-scatter.1
  216.2 64.2 all-gather.7
where the time goes:
time: 378 us; the launch traced here: 377 us
  waiting for transfers between devices  224 us (59%)
  local copies, waits for them, and re-layouts  82.6 us (22%)
  matrix products  29.2 us (8%)
  blocking collectives  15.5 us (4%)
  between operations  14 us (4%)
  other arithmetic  11.7 us (3%)
    all_gather x1, waiting for transfers between devices, shards(): rows = lax.all_gather(got, GROUP, axis=1, tiled=True)  64 us
    reduce_scatter x1, waiting for transfers between devices, shards(): summed = lax.psum_scatter(terms, GROUP, scatter_dimension=0, tiled=True)  60.5 us
    all_gather x1, waiting for transfers between devices, shards(): plane = lax.all_gather(home, GROUP, axis=0, tiled=True)  54 us
    slice x1, local copies, waits for them, and re-layouts, shards(): rows_s = rows[1].reshape(-1, model_width)  53.6 us
    all_gather x1, waiting for transfers between devices, shards(): full_cols = lax.all_gather(stacked, 'expert', axis=0, tiled=True)  44.9 us
    all_to_all x1, blocking collectives, shards(): lax.all_to_all(send, 'expert', split_axis=0, concat_axis=0, tiled=True)  15.5 us
    another operation x1, local copies, waits for them, and re-layouts, shards(): rows_x = rows[0].reshape(-1, model_width)  10 us
    another operation x1, local copies, waits for them, and re-layouts, shards(): rows_s = rows[1].reshape(-1, model_width)  10 us
  transfers between devices with their start and end apart: 4, of which 4 were waited for; matrix products, arithmetic and copies ran while one was open for 4% of the time, Pallas kernels for 0%

commit v1 on v0

--- a/solution.py
+++ b/solution.py
@@ -4,6 +4,11 @@
 from jax.sharding import PartitionSpec as P
 
 GROUP = ("dp", "tensor")
+
+
+def gather_over(value, axis, d):
+    repeated = jnp.stack([value] * lax.axis_size(axis))
+    return jnp.concatenate(lax.all_to_all(repeated, axis, 0, 0), axis=d)
 
 
 def silu_parts(gate_pre):
@@ -45,7 +50,7 @@
     capacity = 5 * count_tok // (2 * experts)
     slots_here = experts * capacity
     stacked = jnp.concatenate([dense_gate, dense_up, dense_down_t], axis=1)
-    full_cols = lax.all_gather(stacked, "expert", axis=0, tiled=True)
+    full_cols = gather_over(stacked, "expert", 0)
     gate_cols = full_cols[:, :hid]
     up_cols = full_cols[:, hid : 2 * hid]
     down_cols = full_cols[:, 2 * hid :]

time: 378 us -> 365 us (0.966)
  waiting for transfers between devices: 224 us -> 194 us
  starting transfers between devices: 0.16 us -> 9.13 us
  matrix products: 29.2 us -> 34.5 us
    all_gather x1 -> x0, waiting for transfers between devices: 44.9 us -> none  [shards(): full_cols = lax.all_gather(stacked, 'expert', axis=0, tiled=True)]
    all_to_all x0 -> x1, waiting for transfers between devices: none -> 29.1 us  [gather_over(): return jnp.concatenate(lax.all_to_all(repeated, axis, 0, 0), axis=d)]
    all_gather x1, waiting for transfers between devices: 54 us -> 43.9 us  [shards(): plane = lax.all_gather(home, GROUP, axis=0, tiled=True)]
    all_to_all x0 -> x1, starting transfers between devices: none -> 9.01 us  [gather_over(): return jnp.concatenate(lax.all_to_all(repeated, axis, 0, 0), axis=d)]
  transfers between devices with their start and end apart: 4 -> 4, of which waited for: 4 -> 4; matrix products, arithmetic and copies ran while one was open for 4% -> 5% of each run, Pallas kernels for 0% -> 0%
where the time goes in v1:
time: 365 us; the launch traced here: 364 us
  waiting for transfers between devices  194 us (53%)
  local copies, waits for them, and re-layouts  84.4 us (23%)
  matrix products  34.5 us (9%)
  blocking collectives  16.3 us (4%)
  between operations  13.9 us (4%)
  other arithmetic  11 us (3%)
  starting transfers between devices  9.13 us (3%)
    all_gather x1, waiting for transfers between devices, shards(): rows = lax.all_gather(got, GROUP, axis=1, tiled=True)  64.2 us
    reduce_scatter x1, waiting for transfers between devices, shards(): summed = lax.psum_scatter(terms, GROUP, scatter_dimension=0, tiled=True)  57 us
    slice x1, local copies, waits for them, and re-layouts, shards(): rows_s = rows[1].reshape(-1, model_width)  53.6 us
    all_gather x1, waiting for transfers between devices, shards(): plane = lax.all_gather(home, GROUP, axis=0, tiled=True)  43.9 us
    all_to_all x1, waiting for transfers between devices, gather_over(): return jnp.concatenate(lax.all_to_all(repeated, axis, 0, 0), axis=d)  29.1 us
    all_to_all x1, blocking collectives, shards(): lax.all_to_all(send, 'expert', split_axis=0, concat_axis=0, tiled=True)  16.3 us
    dot_general x3, matrix products, contract_rows(): lax.dot_general(left_side, right_side, (((0,), (0,)), ((), ())), preferre...  11.2 us
    another operation x1, local copies, waits for them, and re-layouts, shards(): rows_x = rows[0].reshape(-1, model_width)  10 us
  transfers between devices with their start and end apart: 4, of which 4 were waited for; matrix products, arithmetic and copies ran while one was open for 5% of the time, Pallas kernels for 0%

profile of v1, /device:TPU:1, one launch (start us, length us, event | category | flops | bytes accessed | tf_op | source)
XLA Modules:
  0.0 363.5 jit_solution(15917415698415318844)
XLA Ops:
  7.8 1.3 broadcast_select_fusion
  9.3 1.5 fusion.43
  11.9 1.9 stack.4
  13.8 9.0 %all-to-all-start = ((bf16[8,256,768]{2,1,0:T(8,128)(2,1)}), bf16[8,256,768]{2,1,0:T(8,128)(2,1)S(1)}, u32[]{:S(2)}, u32[]{:S(2)}) async-start(bf16[8,256,768]{2,1,0:T(8,128)(2,1)} %stack.4), calls=%async_computation | async-start | bytes 6291456 | tf_op jit(solution)/shard_map/all_to_all | solution.py:11
  22.8 43.9 %all-gather.3.cloned.1.call-done = bf16[512,4224]{1,0:T(8,128)(2,1)} async-done(((bf16[16,4224]{1,0:T(8,128)(2,1)}), bf16[512,4224]{1,0:T(8,128)(2,1)}) %all-gather.3.cloned.1.call-update) | async-done | bytes 4325392 | tf_op jit(solution)/shard_map/all_gather | solution.py:61
  68.0 29.1 %all-to-all-done = bf16[8,256,768]{2,1,0:T(8,128)(2,1)S(1)} async-done(((bf16[8,256,768]{2,1,0:T(8,128)(2,1)}), bf16[8,256,768]{2,1,0:T(8,128)(2,1)S(1)}, u32[]{:S(2)}, u32[]{:S(2)}) %all-to-all-start) | async-done | bytes 3145760 | tf_op jit(solution)/shard_map/all_to_all | solution.py:11
  97.0 2.5 fusion.16
  106.0 2.6 pad_maximum_fusion
  110.9 1.9 convolution_convert_fusion.4
  116.3 1.7 stack_reshape.6
  119.4 16.3 %all_to_all.10 = bf16[8,2,5,2048]{3,1,2,0:T(2,128)(2,1)} all-to-all(bf16[8,2,5,2048]{3,1,2,0:T(2,128)(2,1)S(1)} %copy.25), channel_id=1, replica_groups=mesh['dp'=8,'expert'=8,'tensor'=4] {'expert'}, dimensions={0} | all-to-all | bytes 655360 | tf_op jit(solution)/shard_map/all_to_all | solution.py:103
  135.8 57.0 %reduce-scatter.2.cloned.1.call-done = bf16[16,4096]{1,0:T(8,128)(2,1)} async-done(((bf16[512,4096]{1,0:T(8,128)(2,1)}), bf16[16,4096]{1,0:T(8,128)(2,1)}) %reduce-scatter.2.cloned.1.call-update) | async-done | bytes 131088 | tf_op jit(solution)/shard_map/reduce_scatter | solution.py:75
  192.8 1.5 slice.86
  194.3 1.5 multiply_convert_fusion.14
  195.8 64.2 %all-gather.5.cloned.1.call-done = bf16[2,256,5,2048]{3,0,2,1:T(2,128)(2,1)} async-done(((bf16[2,8,5,2048]{3,0,2,1:T(2,128)(2,1)}), bf16[2,256,5,2048]{3,0,2,1:T(2,128)(2,1)}) %all-gather.5.cloned.1.call-update) | async-done | bytes 10485776 | tf_op jit(solution)/shard_map/all_gather | solution.py:105
  260.0 53.6 %slice_reduce_fusion = (bf16[256,5,2048]{2,1,0:T(8,128)(2,1)}, bf16[256,5,2048]{2,1,0:T(8,128)(2,1)}) fusion(bf16[2,256,5,2048]{3,0,2,1:T(2,128)(2,1)} %all-gather.5.cloned.1.call-done), kind=kLoop, calls=%fused_computation | loop fusion | bytes 20971520 | tf_op jit(solution)/shard_map/slice | solution.py:107
  313.6 10.0 %reshape_squeeze.6 = bf16[1280,2048]{1,0:T(8,128)(2,1)} reshape(bf16[256,5,2048]{2,1,0:T(8,128)(2,1)} %get-tuple-element.18) | data formatting | bytes 10485760 | tf_op jit(solution)/shard_map/reshape;squeeze | solution.py:106
  323.7 5.2 %fusion.24 = f32[1280,256]{1,0:T(8,128)} fusion(bf16[1280,2048]{1,0:T(8,128)(2,1)} %reshape_squeeze.6, bf16[2048,768]{1,0:T(8,128)(2,1)S(1)} %bitcast.24), kind=kOutput, calls=%fused_computation.38 | convolution fusion | flops 1342177280 | bytes 7602176 | tf_op jit(solution)/shard_map/dot_general | solution.py:32
  328.9 2.6 fusion.21
  331.5 10.0 %reshape_squeeze.7 = bf16[1280,2048]{1,0:T(8,128)(2,1)} reshape(bf16[256,5,2048]{2,1,0:T(8,128)(2,1)} %get-tuple-element.17) | data formatting | bytes 10485760 | tf_op jit(solution)/shard_map/reshape;squeeze | solution.py:107
  341.5 4.2 %fusion.27 = f32[1280,256]{1,0:T(8,128)S(1)} fusion(bf16[1280,2048]{1,0:T(8,128)(2,1)} %reshape_squeeze.7, bf16[2048,768]{1,0:T(8,128)(2,1)S(1)} %bitcast.26), kind=kOutput, calls=%fused_computation.41 | convolution fusion | flops 1342177280 | bytes 7602176 | tf_op jit(solution)/shard_map/dot_general | solution.py:40
  345.8 5.4 %fusion.4 = bf16[1,2048,256]{2,1,0:T(8,128)(2,1)} fusion(bf16[1280,2048]{1,0:T(8,128)(2,1)} %reshape_squeeze.7, f32[1280,256]{1,0:T(8,128)S(1)} %copy-done.7, f32[1280,256]{1,0:T(8,128)S(1)} %copy-done.6), kind=kOutput, calls=%fused_computation.14 | convolution fusion | flops 1344667648 | bytes 8912896 | tf_op jit(solution)/shard_map/dot_general | solution.py:20
  351.2 2.9 fusion.3
  354.0 3.0 fusion.2
  (56 shorter events, 16.8 us)
Async XLA Ops:
  7.2 59.6 %all-gather.3.cloned.1.call-start = ((), (), s32[]{:S(2)}) async-start(), calls=%async_computation.3 | async-start | bytes 4460544 | tf_op jit(solution)/shard_map/all_gather | solution.py:61
  13.8 83.3 %all-to-all-start = ((bf16[8,256,768]{2,1,0:T(8,128)(2,1)}), bf16[8,256,768]{2,1,0:T(8,128)(2,1)S(1)}, u32[]{:S(2)}, u32[]{:S(2)}) async-start(bf16[8,256,768]{2,1,0:T(8,128)(2,1)} %stack.4), calls=%async_computation | async-start | bytes 6291456 | tf_op jit(solution)/shard_map/all_to_all | solution.py:11
  22.8 170.0 %reduce-scatter.2.cloned.1.call-start = ((), (), s32[]{:S(2)}) async-start(), calls=%async_computation.4 | async-start | bytes 4325376 | tf_op jit(solution)/shard_map/reduce_scatter | solution.py:75
  97.0 2.9 copy-start.4
  108.5 0.7 copy-start.5
  108.5 0.9 copy-start.3
  108.5 1.0 copy-start.1
  108.5 5.2 %copy-start.2 = (bf16[16,2048]{1,0:T(8,128)(2,1)S(1)}, bf16[16,2048]{1,0:T(8,128)(2,1)}, u32[]{:S(2)}) copy-start(bf16[16,2048]{1,0:T(8,128)(2,1)} %param.9) | copy-start | bytes 196612
  108.6 151.5 %all-gather.5.cloned.1.call-start = ((), (), s32[]{:S(2)}) async-start(), calls=%async_computation.5 | async-start | bytes 10813440 | tf_op jit(solution)/shard_map/all_gather | solution.py:105
  323.7 5.2 %copy-start = (bf16[1280,2048]{1,0:T(8,128)(2,1)S(1)}, bf16[1280,2048]{1,0:T(8,128)(2,1)}, u32[]{:S(2)}) copy-start(bf16[1280,2048]{1,0:T(8,128)(2,1)} %reshape_squeeze.6) | copy-start | bytes 15728644
  341.5 4.2 %copy-start.6 = (f32[1280,256]{1,0:T(8,128)S(1)}, f32[1280,256]{1,0:T(8,128)}, u32[]{:S(2)}) copy-start(f32[1280,256]{1,0:T(8,128)} %fusion.24) | copy-start | bytes 3932164
  341.5 4.2 %copy-start.7 = (f32[1280,256]{1,0:T(8,128)S(1)}, f32[1280,256]{1,0:T(8,128)}, u32[]{:S(2)}) copy-start(f32[1280,256]{1,0:T(8,128)} %fusion.21) | copy-start | bytes 3932164
  341.5 9.6 %slice-start = ((s8[5242880]{0:T(1024)(128)(4,1)}), s8[4194304]{0:T(1024)(128)(4,1)S(1)}, s32[]{:S(2)}) async-start(s8[5242880]{0:T(1024)(128)(4,1)} %bitcast.27), calls=%async_computation.6 | async-start | bytes 8388608
  345.8 5.4 %slice-start.1 = ((s8[5242880]{0:T(1024)(128)(4,1)}), s8[1048576]{0:T(1024)(128)(4,1)S(1)}, s32[]{:S(2)}) async-start(s8[5242880]{0:T(1024)(128)(4,1)} %bitcast.27), calls=%async_computation.7 | async-start | bytes 2097152
Sparse Core Ops, SparseCore 0:
  11.2 55.5 all-gather.2
  108.7 84.0 reduce-scatter.1
  195.7 64.3 all-gather.4
